TPU v7x, 32 devices: a whole 2x2x4 slice. The times are simulated.
32 devices in a mesh: groups: 2 (over y), ctx: 4 (over x, core), head: 4 (over z).
Axes of the slice: x: 2, y: 2, z: 4, core: 2. Of those that a mesh axis runs over, the one named last changes fastest.
Arguments:
- span_query: bfloat16 [4, 128, 64, 128], P('groups', 'ctx', 'head'), parts along dimension 0, may hold values from -5 to 5
- span_key: bfloat16 [4, 128, 8, 128], P('groups', 'ctx', 'head'), parts along dimension 0, may hold values from -15 to 15
- span_value: bfloat16 [4, 128, 8, 128], P('groups', 'ctx', 'head'), parts along dimension 0, may hold values from -6 to 6
- prefix_key: bfloat16 [64, 128, 8, 128], P(('groups', 'ctx'), None, 'head'), parts along dimension 0, may hold values from -15 to 15
- prefix_value: bfloat16 [64, 128, 8, 128], P(('groups', 'ctx'), None, 'head'), parts along dimension 0, may hold values from -6 to 6
- page_table: int32 [4, 16], P('groups', 'ctx'), parts along dimension 0, may hold values from 0 to 7, as said below
- decode_query: bfloat16 [8, 32, 64, 128], P('groups', 'ctx', 'head'), parts along dimension 0, may hold values from -5 to 5
- decode_key: bfloat16 [8, 32, 8, 128], P('groups', 'ctx', 'head'), parts along dimension 0, may hold values from -15 to 15
- decode_value: bfloat16 [8, 32, 8, 128], P('groups', 'ctx', 'head'), parts along dimension 0, may hold values from -6 to 6
- sample_prompt: int32 [64], P('groups'), parts along dimension 0, may hold values from 0 to 1, as said below
- out_weight: bfloat16 [8192, 8192], P('head', 'ctx'), may hold values from -0.25 to 0.25
Outputs:
- span_out: bfloat16 [4, 128, 8192], P('groups', None, 'ctx'), parts along dimension 0
- decode_out: bfloat16 [8, 32, 8192], P('groups', None, 'ctx'), parts along dimension 0
There are 2 independent parts, one for each index of `groups`. A program takes and returns all parts, laid end to end along the dimension named above; an argument that names none is the same for every part. Nothing has to cross between parts.
Inputs may be any that keep to these rules, and one draw needn't show every extreme that they name: `page_table`: within each block of 4 columns (one index of ctx) the entries of both prompts together are a permutation of 0 to 7. `sample_prompt`: every prompt has exactly 16 samples.
All inputs are finite; a program needn't handle non-finite values.
Results may differ from a plain program's by a relative error of at most 0.0075.
Values may be sent and summed in bfloat16 or wider, within the bound.
No kernel may reach another device: no remote copies, remote signals or barrier semaphores. Data moves between devices by JAX's collectives and lax.ppermute only.
A program may use at most 64 MiB of HBM per device.

v0:
```python
import math
import jax
import jax.numpy as jnp
from jax import lax
from jax.sharding import PartitionSpec as P

negative_floor = -1e30


def absorb(softmax_state, queries, key_rows, value_rows, allowed):
    running_max, running_sum, weighted = softmax_state
    scores = jnp.einsum("brd,bnd->brn", queries, key_rows, preferred_element_type=jnp.float32) * (
        1.0 / math.sqrt(queries.shape[-1])
    )
    if allowed is not None:
        scores = jnp.where(allowed, scores, negative_floor)
    new_max = jnp.maximum(running_max, jnp.max(scores, axis=-1))
    factor = jnp.exp(running_max - new_max)
    weights = jnp.exp(scores - new_max[..., None])
    running_sum = running_sum * factor + jnp.sum(weights, axis=-1)
    weighted = weighted * factor[..., None] + jnp.einsum(
        "brn,bnd->brd", weights.astype(jnp.bfloat16), value_rows, preferred_element_type=jnp.float32
    )
    return (new_max, running_sum, weighted)


def sweep(softmax_state, queries, key_rows, value_rows, block_width):
    total_keys = key_rows.shape[1]
    block_width = math.gcd(total_keys, block_width)

    def one_block(state_in, block_start):
        key_block = lax.dynamic_slice_in_dim(key_rows, block_start, block_width, 1)
        value_block = lax.dynamic_slice_in_dim(value_rows, block_start, block_width, 1)
        return (absorb(state_in, queries, key_block, value_block, None), None)

    starts = jnp.arange(total_keys // block_width, dtype=jnp.int32) * block_width
    softmax_state, unused = lax.scan(one_block, softmax_state, starts)
    return softmax_state


def empty_state(head_batch, row_count, head_depth):
    return (
        jnp.full((head_batch, row_count), negative_floor, jnp.float32),
        jnp.zeros((head_batch, row_count), jnp.float32),
        jnp.zeros((head_batch, row_count, head_depth), jnp.float32),
    )


def own_steps(softmax_state, queries_five, own_key, own_value):
    running_max, running_sum, weighted = softmax_state
    key_rows = own_key.transpose(2, 1, 0, 3)
    value_rows = own_value.transpose(2, 1, 0, 3)
    scores = jnp.einsum(
        "ktsgd,ksud->ktsgu", queries_five, key_rows, preferred_element_type=jnp.float32
    ) * (1.0 / math.sqrt(queries_five.shape[-1]))
    step_total = queries_five.shape[1]
    step_ids = jnp.arange(step_total, dtype=jnp.int32)
    allowed = (step_ids[None, :] <= step_ids[:, None])[None, :, None, None, :]
    scores = jnp.where(allowed, scores, negative_floor)
    new_max = jnp.maximum(running_max, jnp.max(scores, axis=-1))
    factor = jnp.exp(running_max - new_max)
    weights = jnp.exp(scores - new_max[..., None])
    running_sum = running_sum * factor + jnp.sum(weights, axis=-1)
    weighted = weighted * factor[..., None] + jnp.einsum(
        "ktsgu,ksud->ktsgd",
        weights.astype(jnp.bfloat16),
        value_rows,
        preferred_element_type=jnp.float32,
    )
    return (weighted / running_sum[..., None]).astype(jnp.bfloat16)


def shards(
    span_query,
    span_key,
    span_value,
    prefix_key,
    prefix_value,
    page_table,
    decode_query,
    decode_key,
    decode_value,
    sample_prompt,
    out_weight,
):
    prompts, span_dev, heads_dev, head_depth = span_query.shape
    kv_heads = span_key.shape[2]
    group_size = heads_dev // kv_heads
    steps_count = decode_query.shape[0]
    samples_dev = decode_query.shape[1]
    head_batch = prompts * kv_heads
    ctx_index = lax.axis_index("ctx")
    slot_rows = page_table.reshape(-1)
    local_keys = (
        jnp.take(prefix_key, slot_rows, axis=0)
        .reshape(prompts, -1, kv_heads, head_depth)
        .transpose(0, 2, 1, 3)
    )
    local_values = (
        jnp.take(prefix_value, slot_rows, axis=0)
        .reshape(prompts, -1, kv_heads, head_depth)
        .transpose(0, 2, 1, 3)
    )
    span_rows = (
        span_query.reshape(prompts, span_dev, kv_heads, group_size, head_depth)
        .transpose(0, 2, 1, 3, 4)
        .reshape(head_batch, span_dev * group_size, head_depth)
    )
    span_keys_all, span_values_all = (
        lax.all_gather(span_key, "ctx", axis=1, tiled=True),
        lax.all_gather(span_value, "ctx", axis=1, tiled=True),
    )
    span_total = span_keys_all.shape[1]
    span_key_rows = span_keys_all.transpose(0, 2, 1, 3).reshape(head_batch, span_total, head_depth)
    span_value_rows = span_values_all.transpose(0, 2, 1, 3).reshape(
        head_batch, span_total, head_depth
    )
    query_pos = (
        ctx_index * span_dev + jnp.arange(span_dev * group_size, dtype=jnp.int32) // group_size
    )
    causal = (jnp.arange(span_total, dtype=jnp.int32)[None, :] <= query_pos[:, None])[None]
    decode_five = decode_query.reshape(
        steps_count, samples_dev, kv_heads, group_size, head_depth
    ).transpose(2, 0, 1, 3, 4)
    prefill_state = empty_state(head_batch, span_dev * group_size, head_depth)
    prompt_keys_all, prompt_values_all = (
        lax.all_gather(local_keys, "ctx", axis=2, tiled=True),
        lax.all_gather(local_values, "ctx", axis=2, tiled=True),
    )
    prefix_len = prompt_keys_all.shape[2]
    key_rows = prompt_keys_all.reshape(head_batch, prefix_len, head_depth)
    value_rows = prompt_values_all.reshape(head_batch, prefix_len, head_depth)
    prefill_state = sweep(prefill_state, span_rows, key_rows, value_rows, 2048)
    decode_flat = decode_five.reshape(kv_heads, -1, head_depth)
    decode_batch = jnp.broadcast_to(decode_flat[None], (prompts,) + decode_flat.shape).reshape(
        head_batch, -1, head_depth
    )
    decode_state = empty_state(head_batch, decode_flat.shape[1], head_depth)
    decode_state = sweep(decode_state, decode_batch, key_rows, value_rows, 2048)
    decode_state = sweep(decode_state, decode_batch, span_key_rows, span_value_rows, span_total)
    own_prompts = lax.dynamic_slice_in_dim(sample_prompt, ctx_index * samples_dev, samples_dev)
    chosen = (
        own_prompts[None, None, None, :, None]
        == jnp.arange(prompts, dtype=jnp.int32)[:, None, None, None, None]
    )

    def select_prompt(member):
        shaped = member.reshape(
            (prompts, kv_heads, steps_count, samples_dev, group_size) + member.shape[2:]
        )
        select_mask = chosen.reshape(chosen.shape + (1,) * (shaped.ndim - 5))
        return jnp.sum(jnp.where(select_mask, shaped, 0.0), axis=0)

    decode_state = tuple((select_prompt(member) for member in decode_state))
    prefill_state = absorb(prefill_state, span_rows, span_key_rows, span_value_rows, causal)
    span_mixed = (prefill_state[2] / prefill_state[1][..., None]).astype(jnp.bfloat16)
    span_attn = (
        span_mixed.reshape(prompts, kv_heads, span_dev, group_size, head_depth)
        .transpose(0, 2, 1, 3, 4)
        .reshape(prompts * span_dev, heads_dev * head_depth)
    )
    decode_mixed = own_steps(decode_state, decode_five, decode_key, decode_value)
    decode_attn = decode_mixed.transpose(1, 2, 0, 3, 4).reshape(
        steps_count * samples_dev, heads_dev * head_depth
    )
    rows_local = jnp.concatenate([span_attn, decode_attn], axis=0)
    projected = jnp.dot(
        lax.all_gather(rows_local, "ctx", axis=0, tiled=True),
        out_weight,
        preferred_element_type=jnp.float32,
    )
    share = lax.psum_scatter(projected, "head", scatter_dimension=0, tiled=True).astype(
        jnp.bfloat16
    )
    summed = lax.all_gather(share, "head", axis=0, tiled=True)
    rows_dev = rows_local.shape[0]
    blocks_by_ctx = summed.reshape(-1, rows_dev, summed.shape[-1])
    ctx_count = blocks_by_ctx.shape[0]
    span_out = (
        blocks_by_ctx[:, : prompts * span_dev]
        .reshape(ctx_count, prompts, span_dev, -1)
        .transpose(1, 0, 2, 3)
        .reshape(prompts, ctx_count * span_dev, -1)
    )
    decode_out = (
        blocks_by_ctx[:, prompts * span_dev :]
        .reshape(ctx_count, steps_count, samples_dev, -1)
        .transpose(1, 0, 2, 3)
        .reshape(steps_count, ctx_count * samples_dev, -1)
    )
    return (span_out, decode_out)


def solution(mesh):
    return jax.shard_map(
        shards,
        mesh=mesh,
        in_specs=(
            P("groups", "ctx", "head", None),
            P("groups", "ctx", "head", None),
            P("groups", "ctx", "head", None),
            P(("groups", "ctx"), None, "head", None),
            P(("groups", "ctx"), None, "head", None),
            P("groups", "ctx"),
            P("groups", "ctx", "head", None),
            P("groups", "ctx", "head", None),
            P("groups", "ctx", "head", None),
            P("groups"),
            P("head", "ctx"),
        ),
        out_specs=(P("groups", None, "ctx"), P("groups", None, "ctx")),
        check_vma=False,
    )
```

profile of v0, /device:TPU:0, one launch (start us, length us, event | category | flops | bytes accessed | tf_op | source)
XLA Modules:
  0.0 230.2 jit_solution(950019936043663763)
XLA Ops:
  7.2 0.0 copy-start
  7.2 0.0 copy-start.8
  7.2 0.0 all-gather.5.cloned.1.call-start
  7.3 0.8 reshape.229
  8.1 0.2 copy-done
  8.3 1.6 gather_fusion
  9.9 2.6 %gather_fusion.1 = bf16[8,128,2,128]{3,2,1,0:T(2,128)(2,1)S(1)} fusion(bf16[8,128,2,128]{3,2,1,0:T(2,128)(2,1)} %param.17, s32[1024]{0:T(1024)S(1)} %pad_clamp_fusion), kind=kCustom, calls=%fused_computation.1.clone | custom fusion | bytes 1048608 | tf_op jit(solution)/shard_map/jit(_take)/gather | solution.py:100
  12.6 1.0 broadcast_select_fusion.1
  13.6 0.9 copy.135
  14.4 0.0 all-gather.5.cloned.1.call-update
  14.5 0.0 all-gather.7.cloned.1.call-start
  14.5 0.9 copy.134
  15.4 0.0 all-gather.7.cloned.1.call-update
  15.4 0.0 all-gather.9.cloned.1.call-start
  15.5 6.7 %all_gather.20 = bf16[2,128,2,128]{3,2,1,0:T(2,128)(2,1)S(1)} all-gather(bf16[2,32,2,128]{3,2,1,0:T(2,128)(2,1)} %param.14), channel_id=1, replica_groups=mesh['groups'=2,'ctx'=4,'head'=4] {'ctx'}, dimensions={1}, use_global_device_ids=true | all-gather | bytes 163840 | tf_op jit(solution)/shard_map/all_gather | solution.py:110
  22.2 0.9 copy.89
  23.2 0.2 fusion.56
  23.4 6.2 %all_gather.21 = bf16[2,128,2,128]{3,2,1,0:T(2,128)(2,1)S(1)} all-gather(bf16[2,32,2,128]{3,2,1,0:T(2,128)(2,1)S(1)} %copy-done.9), channel_id=1, replica_groups=mesh['groups'=2,'ctx'=4,'head'=4] {'ctx'}, dimensions={1}, use_global_device_ids=true | all-gather | bytes 163840 | tf_op jit(solution)/shard_map/all_gather | solution.py:111
  29.8 0.7 reduce_max.56
  30.5 0.1 dynamic_slice.22
  30.6 0.5 iota_compare_fusion.2
  31.1 2.0 fusion.57
  33.0 0.2 fusion.58
  33.3 7.3 %all-gather.5.cloned.1.call-done = bf16[2,2,2048,128]{3,2,1,0:T(8,128)(2,1)} async-done(((bf16[2,2,512,128]{3,2,1,0:T(8,128)(2,1)}), bf16[2,2,2048,128]{3,2,1,0:T(8,128)(2,1)}) %all-gather.5.cloned.1.call-update) | async-done | bytes 2097168 | tf_op jit(solution)/shard_map/all_gather | solution.py:127
  40.6 2.9 %bitcast_reduce_fusion.1 = (f32[4,256]{1,0:T(4,128)S(1)}, f32[4,2048,256]{2,1,0:T(8,128)S(1)}) fusion(bf16[4,2048,128]{2,1,0:T(8,128)(2,1)} %bitcast.123, bf16[4,256,128]{2,1,0:T(8,128)(2,1)S(1)} %bitcast.131), kind=kOutput, calls=%fused_computation.6 | convolution fusion | flops 541064192 | bytes 10752000 | tf_op jit(solution)/shard_map/while/body/eval_jaxpr/brd,bnd->brn/dot_general | solution.py:12
  43.5 0.1 fusion.34
  43.6 3.4 %copy-done.1 = f32[4,2048,256]{2,1,0:T(8,128)} copy-done((f32[4,2048,256]{2,1,0:T(8,128)}, f32[4,2048,256]{2,1,0:T(8,128)S(1)}, u32[]{:S(2)}) %copy-start.1) | copy-done | bytes 8388632
  47.0 1.4 fusion.2
  48.4 0.6 multiply_add_fusion
  49.0 5.1 %bitcast_reduce_fusion = (f32[4,256]{1,0:T(4,128)}, f32[4,2048,256]{2,1,0:T(8,128)}) fusion(bf16[4,2048,128]{2,1,0:T(8,128)(2,1)S(1)} %bitcast.124, bf16[4,256,128]{2,1,0:T(8,128)(2,1)S(1)} %bitcast.129), kind=kOutput, calls=%fused_computation.3 | convolution fusion | flops 541064192 | bytes 10752000 | tf_op jit(solution)/shard_map/while/body/eval_jaxpr/brd,bnd->brn/dot_general | solution.py:12
  54.1 11.3 %all-gather.7.cloned.1.call-done = bf16[2,2,2048,128]{3,2,1,0:T(8,128)(2,1)} async-done(((bf16[2,2,512,128]{3,2,1,0:T(8,128)(2,1)}), bf16[2,2,2048,128]{3,2,1,0:T(8,128)(2,1)}) %all-gather.7.cloned.1.call-update) | async-done | bytes 2097168 | tf_op jit(solution)/shard_map/all_gather | solution.py:128
  65.4 5.2 %fusion.25 = f32[4,256,128]{2,1,0:T(8,128)S(1)} fusion(bf16[4,2048,128]{2,1,0:T(8,128)(2,1)} %bitcast.125, f32[4,2048,256]{2,1,0:T(8,128)} %copy-done.1, f32[4,256]{1,0:T(4,128)S(1)} %get-tuple-element.62, f32[4,256]{1,0:T(4,128)S(1)} %get-tuple-element.48, f32[4,256]{1,0:T(4,128)S(1)} %get-tuple-element.60), kind=kOutput, calls=%fused_computation.27 | convolution fusion | flops 543424512 | bytes 11022336 | tf_op jit(solution)/shard_map/while/body/eval_jaxpr/brn,bnd->brd/dot_general | solution.py:21
  70.6 0.3 fusion.28
  71.0 0.7 copy.136
  71.7 1.1 reshape.239
  72.8 1.3 fusion.54
  74.1 0.7 max.91
  74.8 4.8 %fusion.4 = f32[4,256]{1,0:T(4,128)S(1)} fusion(f32[4,2048,256]{2,1,0:T(8,128)} %get-tuple-element.84, f32[4,256]{1,0:T(4,128)S(1)} %get-tuple-element.71), kind=kLoop, calls=%fused_computation.10 | loop fusion | flops 6290432 | bytes 8396800 | tf_op jit(solution)/shard_map/while/body/eval_jaxpr/reduce_sum | solution.py:20
  79.5 0.7 reduce_sum.94
  80.3 0.1 fusion.36
  80.3 0.7 reduce_sum.96
  81.1 1.1 select_reduce_fusion.1
  82.1 0.8 copy_maximum_fusion
  82.9 1.0 fusion.43
  83.9 0.8 bitcast_add_fusion
  84.8 4.6 %fusion.22 = f32[4,256,128]{2,1,0:T(8,128)S(1)} fusion(bf16[4,2048,128]{2,1,0:T(8,128)(2,1)S(1)} %bitcast.126, f32[4,2048,256]{2,1,0:T(8,128)} %get-tuple-element.84, f32[4,256]{1,0:T(4,128)S(1)} %get-tuple-element.71, f32[4,256]{1,0:T(4,128)S(1)} %get-tuple-element.59, f32[4,256]{1,0:T(4,128)} %get-tuple-element.70), kind=kOutput, calls=%fused_computation.26 | convolution fusion | flops 543424512 | bytes 11022336 | tf_op jit(solution)/shard_map/while/body/eval_jaxpr/brn,bnd->brd/dot_general | solution.py:21
  89.3 0.3 convolution_add_fusion
  89.6 0.1 select_reduce_fusion
  89.8 0.3 fusion.31
  90.1 0.1 reshape.243
  90.2 0.8 pad_maximum_fusion
  91.0 0.0 all-gather.9.cloned.1.call-update
  91.0 0.3 reduce-scatter.2.cloned.1.call-start
  91.3 19.5 %all-gather.9.cloned.1.call-done = bf16[384,2048]{1,0:T(8,128)(2,1)} async-done(((bf16[96,2048]{1,0:T(8,128)(2,1)}), bf16[384,2048]{1,0:T(8,128)(2,1)}) %all-gather.9.cloned.1.call-update) | async-done | bytes 1572880 | tf_op jit(solution)/shard_map/all_gather | solution.py:168
  110.8 8.9 %fusion.59 = f32[384,2048]{1,0:T(8,128)} fusion(bf16[384,2048]{1,0:T(8,128)(2,1)} %all-gather.9.cloned.1.call-done, bf16[2048,2048]{1,0:T(8,128)(2,1)} %param.23), kind=kOutput, calls=%fused_computation.93 | convolution fusion | flops 3221225472 | bytes 13107200 | tf_op jit(solution)/shard_map/dot_general | solution.py:167
  119.7 0.0 reduce-scatter.2.cloned.1.call-update
  119.8 0.0 all-gather.11.cloned.1.call-start
  119.8 60.4 %reduce-scatter.2.cloned.1.call-done = f32[96,2048]{1,0:T(8,128)} async-done(((f32[384,2048]{1,0:T(8,128)}), f32[96,2048]{1,0:T(8,128)}) %reduce-scatter.2.cloned.1.call-update) | async-done | bytes 786448 | tf_op jit(solution)/shard_map/reduce_scatter | solution.py:172
  180.2 1.9 convert_element_type.35
  182.1 0.0 all-gather.11.cloned.1.call-update
  182.1 37.3 %all-gather.11.cloned.1.call-done = bf16[384,2048]{1,0:T(8,128)(2,1)} async-done(((bf16[96,2048]{1,0:T(8,128)(2,1)}), bf16[384,2048]{1,0:T(8,128)(2,1)}) %all-gather.11.cloned.1.call-update) | async-done | bytes 1572880 | tf_op jit(solution)/shard_map/all_gather | solution.py:175
  219.4 1.3 slice.12
  220.7 1.9 copy_bitcast_fusion
  222.6 1.0 copy.103
  (41 shorter events, 0.3 us)
Async XLA Ops:
  7.2 1.2 copy-start
  7.2 23.9 %copy-start.8 = (bf16[4,8,16,128]{3,2,1,0:T(8,128)(2,1)S(1)}, bf16[4,8,16,128]{3,2,1,0:T(8,128)(2,1)}, u32[]{:S(2)}) copy-start(bf16[4,8,16,128]{3,2,1,0:T(8,128)(2,1)} %param.19) | copy-start | bytes 393220
  7.2 16.2 %copy-start.9 = (bf16[2,32,2,128]{3,2,1,0:T(2,128)(2,1)S(1)}, bf16[2,32,2,128]{3,2,1,0:T(2,128)(2,1)}, u32[]{:S(2)}) copy-start(bf16[2,32,2,128]{3,2,1,0:T(2,128)(2,1)} %param.15) | copy-start | bytes 98308
  7.2 22.5 %copy-start.6 = (bf16[2,32,16,128]{3,2,1,0:T(8,128)(2,1)S(1)}, bf16[2,32,16,128]{3,2,1,0:T(8,128)(2,1)}, u32[]{:S(2)}) copy-start(bf16[2,32,16,128]{3,2,1,0:T(8,128)(2,1)} %param.13) | copy-start | bytes 786436
  7.2 23.3 %copy-start.14 = (s32[32]{0:T(128)S(1)}, s32[32]{0:T(128)}, u32[]{:S(2)}) copy-start(s32[32]{0:T(128)} %param.22) | copy-start | bytes 388
  7.2 23.9 %copy-start.12 = (bf16[4,8,2,128]{3,2,1,0:T(2,128)(2,1)S(1)}, bf16[4,8,2,128]{3,2,1,0:T(2,128)(2,1)}, u32[]{:S(2)}) copy-start(bf16[4,8,2,128]{3,2,1,0:T(2,128)(2,1)} %param.20) | copy-start | bytes 49156
  7.2 33.4 %all-gather.5.cloned.1.call-start = ((), (), s32[]{:S(2)}) async-start(), calls=%async_computation.1 | async-start | bytes 2621440 | tf_op jit(solution)/shard_map/all_gather | solution.py:127
  14.5 50.9 %all-gather.7.cloned.1.call-start = ((), (), s32[]{:S(2)}) async-start(), calls=%async_computation.2 | async-start | bytes 2621440 | tf_op jit(solution)/shard_map/all_gather | solution.py:128
  15.4 95.4 %all-gather.9.cloned.1.call-start = ((), (), s32[]{:S(2)}) async-start(), calls=%async_computation.3 | async-start | bytes 1966080 | tf_op jit(solution)/shard_map/all_gather | solution.py:168
  33.3 15.1 %copy-start.4 = (f32[4,256,128]{1,2,0:T(8,128)}, f32[4,256,128]{1,2,0:T(8,128)S(1)}, u32[]{:S(2)}) copy-start(f32[4,256,128]{1,2,0:T(8,128)S(1)} %get-tuple-element.90) | copy-start | bytes 1572868
  43.5 3.5 %copy-start.1 = (f32[4,2048,256]{2,1,0:T(8,128)}, f32[4,2048,256]{2,1,0:T(8,128)S(1)}, u32[]{:S(2)}) copy-start(f32[4,2048,256]{2,1,0:T(8,128)S(1)} %get-tuple-element.88) | copy-start | bytes 25165828
  43.5 5.5 %copy-start.2 = (bf16[2,2,2048,128]{3,2,1,0:T(8,128)(2,1)S(1)}, bf16[2,2,2048,128]{3,2,1,0:T(8,128)(2,1)}, u32[]{:S(2)}) copy-start(bf16[2,2,2048,128]{3,2,1,0:T(8,128)(2,1)} %all-gather.5.cloned.1.call-done) | copy-start | bytes 6291460
  54.1 16.6 %copy-start.10 = (f32[4,256]{1,0:T(4,128)S(1)}, f32[4,256]{1,0:T(4,128)}, u32[]{:S(2)}) copy-start(f32[4,256]{1,0:T(4,128)} %get-tuple-element.47) | copy-start | bytes 12292
  65.4 5.3 %copy-start.5 = (f32[4,256,128]{1,2,0:T(8,128)S(1)}, f32[4,256,128]{1,2,0:T(8,128)}, u32[]{:S(2)}) copy-start(f32[4,256,128]{1,2,0:T(8,128)} %copy-done.4) | copy-start | bytes 1572868
  70.6 14.2 %copy-start.3 = (bf16[2,2,2048,128]{3,2,1,0:T(8,128)(2,1)S(1)}, bf16[2,2,2048,128]{3,2,1,0:T(8,128)(2,1)}, u32[]{:S(2)}) copy-start(bf16[2,2,2048,128]{3,2,1,0:T(8,128)(2,1)} %all-gather.7.cloned.1.call-done) | copy-start | bytes 6291460
  81.1 8.6 %copy-start.11 = (pred[2,8]{1,0:T(4,128)(4,1)S(1)}, pred[2,8]{1,0:T(4,128)(4,1)}, u32[]{:S(2)}) copy-start(pred[2,8]{1,0:T(4,128)(4,1)} %iota_compare_fusion.2) | copy-start | bytes 52
  81.1 8.7 %copy-start.7 = (f32[2,4,8,8,4]{3,4,1,2,0:T(4,128)S(1)}, f32[2,4,8,8,4]{3,4,1,2,0:T(4,128)}, u32[]{:S(2)}) copy-start(f32[2,4,8,8,4]{3,4,1,2,0:T(4,128)} %get-tuple-element.86) | copy-start | bytes 24580
  81.1 8.7 %copy-start.13 = (bf16[4,8,2,128]{3,2,1,0:T(2,128)(2,1)S(1)}, bf16[4,8,2,128]{3,2,1,0:T(2,128)(2,1)}, u32[]{:S(2)}) copy-start(bf16[4,8,2,128]{3,2,1,0:T(2,128)(2,1)} %param.21) | copy-start | bytes 49156
  91.0 89.2 %reduce-scatter.2.cloned.1.call-start = ((), (), s32[]{:S(2)}) async-start(), calls=%async_computation.4 | async-start | bytes 3932160 | tf_op jit(solution)/shard_map/reduce_scatter | solution.py:172
  119.8 99.6 %all-gather.11.cloned.1.call-start = ((), (), s32[]{:S(2)}) async-start(), calls=%async_computation.5 | async-start | bytes 1966080 | tf_op jit(solution)/shard_map/all_gather | solution.py:175
Sparse Core Ops, SparseCore 0:
  14.6 25.9 all-gather.4
  42.7 22.5 all-gather.6
  91.1 19.6 all-gather.8
  119.9 60.2 reduce-scatter.1
  182.2 37.1 all-gather.10
where the time goes:
time: 231 us; the launch traced here: 230 us
  waiting for transfers between devices  136 us (59%)
  matrix products  30 us (13%)
  local copies, waits for them, and re-layouts  20.6 us (9%)
  other arithmetic  16.2 us (7%)
  between operations  14.1 us (6%)
  blocking collectives  12.9 us (6%)
    reduce_scatter x1, waiting for transfers between devices, shards(): lax.psum_scatter(projected, 'head', scatter_dimension=0, tiled=True)  60.4 us
    all_gather x1, waiting for transfers between devices, shards(): summed = lax.all_gather(share, 'head', axis=0, tiled=True)  37.3 us
    all_gather x1, waiting for transfers between devices, shards(): lax.all_gather(rows_local, 'ctx', axis=0, tiled=True)  19.5 us
    all_gather x1, waiting for transfers between devices, shards(): lax.all_gather(local_values, 'ctx', axis=2, tiled=True)  11.3 us
    dot_general x4, matrix products, absorb(): jnp.einsum('brn,bnd->brd', weights.astype(jnp.bfloat16), value_rows, pref...  10.4 us
    dot_general x1, matrix products, shards(): jnp.dot(lax.all_gather(rows_local, 'ctx', axis=0, tiled=True), out_weight...  8.94 us
    dot_general x4, matrix products, absorb(): jnp.einsum('brd,bnd->brn', queries, key_rows, preferred_element_type=jnp....  8.4 us
    all_gather x1, waiting for transfers between devices, shards(): lax.all_gather(local_keys, 'ctx', axis=2, tiled=True)  7.31 us
  transfers between devices with their start and end apart: 5, of which 5 were waited for; matrix products, arithmetic and copies ran while one was open for 7% of the time, Pallas kernels for 0%

commit v1 on v0

--- a/solution.py
+++ b/solution.py
@@ -172,7 +172,12 @@
     share = lax.psum_scatter(projected, "head", scatter_dimension=0, tiled=True).astype(
         jnp.bfloat16
     )
-    summed = lax.all_gather(share, "head", axis=0, tiled=True)
+    ring = [share]
+    for hop in range(3):
+        ring.append(lax.ppermute(ring[-1], "head", [(dev, (dev + 1) % 4) for dev in range(4)]))
+    summed = jnp.roll(
+        jnp.concatenate(ring[::-1], axis=0), (lax.axis_index("head") + 1) * ring[0].shape[0], axis=0
+    )
     rows_dev = rows_local.shape[0]
     blocks_by_ctx = summed.reshape(-1, rows_dev, summed.shape[-1])
     ctx_count = blocks_by_ctx.shape[0]

time: 231 us -> 224 us (0.970)
  local copies, waits for them, and re-layouts: 20.6 us -> 15.1 us
    all_gather x1 -> x0, waiting for transfers between devices: 37.3 us -> none  [shards(): summed = lax.all_gather(share, 'head', axis=0, tiled=True)]
    ppermute x0 -> x3, waiting for transfers between devices: none -> 33.7 us  [shards(): lax.ppermute(ring[-1], 'head', [(dev, (dev + 1) % 4) for dev in range(4)])]
    all_gather x1, waiting for transfers between devices: 11.3 us -> 14.2 us  [shards(): lax.all_gather(local_values, 'ctx', axis=2, tiled=True)]
  transfers between devices with their start and end apart: 5 -> 7, of which waited for: 5 -> 7; matrix products, arithmetic and copies ran while one was open for 7% -> 6% of each run, Pallas kernels for 0% -> 0%
where the time goes in v1:
time: 224 us; the launch traced here: 223 us
  waiting for transfers between devices  136 us (61%)
  matrix products  29.6 us (13%)
  local copies, waits for them, and re-layouts  15.1 us (7%)
  other arithmetic  14.5 us (6%)
  between operations  14.2 us (6%)
  blocking collectives  12.4 us (6%)
    reduce_scatter x1, waiting for transfers between devices, shards(): lax.psum_scatter(projected, 'head', scatter_dimension=0, tiled=True)  60.4 us
    ppermute x3, waiting for transfers between devices, shards(): lax.ppermute(ring[-1], 'head', [(dev, (dev + 1) % 4) for dev in range(4)])  33.7 us
    all_gather x1, waiting for transfers between devices, shards(): lax.all_gather(rows_local, 'ctx', axis=0, tiled=True)  19.5 us
    all_gather x1, waiting for transfers between devices, shards(): lax.all_gather(local_values, 'ctx', axis=2, tiled=True)  14.2 us
    dot_general x4, matrix products, absorb(): jnp.einsum('brn,bnd->brd', weights.astype(jnp.bfloat16), value_rows, pref...  10.4 us
    dot_general x1, matrix products, shards(): jnp.dot(lax.all_gather(rows_local, 'ctx', axis=0, tiled=True), out_weight...  8.94 us
    all_gather x1, waiting for transfers between devices, shards(): lax.all_gather(local_keys, 'ctx', axis=2, tiled=True)  8.13 us
    dot_general x4, matrix products, absorb(): jnp.einsum('brd,bnd->brn', queries, key_rows, preferred_element_type=jnp....  8.05 us
  transfers between devices with their start and end apart: 7, of which 7 were waited for; matrix products, arithmetic and copies ran while one was open for 6% of the time, Pallas kernels for 0%

profile of v1, /device:TPU:0, one launch (start us, length us, event | category | flops | bytes accessed | tf_op | source)
XLA Modules:
  0.0 223.3 jit_solution(764606031600318337)
XLA Ops:
  7.2 0.0 copy-start
  7.2 0.0 all-gather.4.cloned.1.call-start
  7.2 0.8 reshape.229
  8.1 0.2 copy-done
  8.2 1.6 gather_fusion
  9.8 0.0 copy-start.8
  9.8 0.0 copy-start.7
  9.9 2.7 %gather_fusion.1 = bf16[8,128,2,128]{3,2,1,0:T(2,128)(2,1)S(1)} fusion(bf16[8,128,2,128]{3,2,1,0:T(2,128)(2,1)} %param.17, s32[1024]{0:T(1024)S(1)} %pad_clamp_fusion), kind=kCustom, calls=%fused_computation.1.clone | custom fusion | bytes 1048608 | tf_op jit(solution)/shard_map/jit(_take)/gather | solution.py:100
  12.6 1.0 broadcast_select_fusion.1
  13.6 0.9 copy.131
  14.4 0.0 all-gather.4.cloned.1.call-update
  14.5 0.0 all-gather.6.cloned.1.call-start
  14.5 0.9 copy.130
  15.4 0.0 all-gather.6.cloned.1.call-update
  15.4 0.0 all-gather.8.cloned.1.call-start
  15.5 6.5 %all_gather.17 = bf16[2,128,2,128]{3,2,1,0:T(2,128)(2,1)S(1)} all-gather(bf16[2,32,2,128]{3,2,1,0:T(2,128)(2,1)S(1)} %copy-done.8), channel_id=1, replica_groups=mesh['groups'=2,'ctx'=4,'head'=4] {'ctx'}, dimensions={1}, use_global_device_ids=true | all-gather | bytes 163840 | tf_op jit(solution)/shard_map/all_gather | solution.py:110
  22.1 0.2 fusion.56
  22.3 5.9 %all_gather.18 = bf16[2,128,2,128]{3,2,1,0:T(2,128)(2,1)S(1)} all-gather(bf16[2,32,2,128]{3,2,1,0:T(2,128)(2,1)S(1)} %copy-done.9), channel_id=1, replica_groups=mesh['groups'=2,'ctx'=4,'head'=4] {'ctx'}, dimensions={1}, use_global_device_ids=true | all-gather | bytes 163840 | tf_op jit(solution)/shard_map/all_gather | solution.py:111
  28.3 0.7 reduce_max.56
  29.0 0.1 dynamic_slice.26
  29.1 0.6 iota_compare_fusion.2
  29.7 1.9 fusion.57
  31.7 0.2 fusion.58
  31.9 8.1 %all-gather.4.cloned.1.call-done = bf16[2,2,2048,128]{3,2,1,0:T(8,128)(2,1)} async-done(((bf16[2,2,512,128]{3,2,1,0:T(8,128)(2,1)}), bf16[2,2,2048,128]{3,2,1,0:T(8,128)(2,1)}) %all-gather.4.cloned.1.call-update) | async-done | bytes 2097168 | tf_op jit(solution)/shard_map/all_gather | solution.py:127
  40.0 2.8 %bitcast_reduce_fusion.1 = (f32[4,256]{1,0:T(4,128)S(1)}, f32[4,2048,256]{2,1,0:T(8,128)S(1)}) fusion(bf16[4,2048,128]{2,1,0:T(8,128)(2,1)} %bitcast.123, bf16[4,256,128]{2,1,0:T(8,128)(2,1)S(1)} %bitcast.133), kind=kOutput, calls=%fused_computation.6 | convolution fusion | flops 541064192 | bytes 10752000 | tf_op jit(solution)/shard_map/while/body/eval_jaxpr/brd,bnd->brn/dot_general | solution.py:12
  42.9 0.1 fusion.34
  43.0 1.4 fusion.2
  44.4 2.0 copy-done.1
  46.5 4.7 %bitcast_reduce_fusion = (f32[4,256]{1,0:T(4,128)S(1)}, f32[4,2048,256]{2,1,0:T(8,128)}) fusion(bf16[4,2048,128]{2,1,0:T(8,128)(2,1)S(1)} %bitcast.124, bf16[4,256,128]{2,1,0:T(8,128)(2,1)S(1)} %bitcast.131), kind=kOutput, calls=%fused_computation.3 | convolution fusion | flops 541064192 | bytes 10752000 | tf_op jit(solution)/shard_map/while/body/eval_jaxpr/brd,bnd->brn/dot_general | solution.py:12
  51.2 14.2 %all-gather.6.cloned.1.call-done = bf16[2,2,2048,128]{3,2,1,0:T(8,128)(2,1)} async-done(((bf16[2,2,512,128]{3,2,1,0:T(8,128)(2,1)}), bf16[2,2,2048,128]{3,2,1,0:T(8,128)(2,1)}) %all-gather.6.cloned.1.call-update) | async-done | bytes 2097168 | tf_op jit(solution)/shard_map/all_gather | solution.py:128
  65.4 5.2 %fusion.25 = f32[4,256,128]{2,1,0:T(8,128)S(1)} fusion(bf16[4,2048,128]{2,1,0:T(8,128)(2,1)} %bitcast.125, f32[4,2048,256]{2,1,0:T(8,128)} %copy-done.1, f32[4,256]{1,0:T(4,128)S(1)} %get-tuple-element.62, f32[4,256]{1,0:T(4,128)S(1)} %get-tuple-element.48, f32[4,256]{1,0:T(4,128)S(1)} %get-tuple-element.60), kind=kOutput, calls=%fused_computation.27 | convolution fusion | flops 543424512 | bytes 11022336 | tf_op jit(solution)/shard_map/while/body/eval_jaxpr/brn,bnd->brd/dot_general | solution.py:21
  70.6 0.3 fusion.28
  70.9 0.1 reshape.239
  71.1 0.6 fusion.54
  71.7 0.7 max.91
  72.4 4.9 %fusion.4 = f32[4,256]{1,0:T(4,128)S(1)} fusion(f32[4,2048,256]{2,1,0:T(8,128)} %get-tuple-element.84, f32[4,256]{1,0:T(4,128)S(1)} %get-tuple-element.71), kind=kLoop, calls=%fused_computation.10 | loop fusion | flops 6290432 | bytes 8396800 | tf_op jit(solution)/shard_map/while/body/eval_jaxpr/reduce_sum | solution.py:20
  77.3 0.7 reduce_sum.94
  78.0 0.1 fusion.36
  78.1 0.7 reduce_sum.96
  78.8 1.0 select_reduce_fusion.1
  79.9 0.8 copy_maximum_fusion
  80.6 1.0 fusion.43
  81.7 0.8 bitcast_add_fusion
  82.5 4.6 %fusion.22 = f32[4,256,128]{2,1,0:T(8,128)S(1)} fusion(bf16[4,2048,128]{2,1,0:T(8,128)(2,1)S(1)} %bitcast.126, f32[4,2048,256]{2,1,0:T(8,128)} %get-tuple-element.84, f32[4,256]{1,0:T(4,128)S(1)} %get-tuple-element.71, f32[4,256]{1,0:T(4,128)S(1)} %get-tuple-element.59, f32[4,256]{1,0:T(4,128)} %get-tuple-element.70), kind=kOutput, calls=%fused_computation.26 | convolution fusion | flops 543424512 | bytes 11022336 | tf_op jit(solution)/shard_map/while/body/eval_jaxpr/brn,bnd->brd/dot_general | solution.py:21
  87.1 0.3 convolution_add_fusion
  87.4 0.1 select_reduce_fusion
  87.5 0.3 fusion.31
  87.9 0.1 reshape.243
  88.0 0.8 pad_maximum_fusion
  88.7 0.0 all-gather.8.cloned.1.call-update
  88.8 0.3 reduce-scatter.2.cloned.1.call-start
  89.0 19.5 %all-gather.8.cloned.1.call-done = bf16[384,2048]{1,0:T(8,128)(2,1)} async-done(((bf16[96,2048]{1,0:T(8,128)(2,1)}), bf16[384,2048]{1,0:T(8,128)(2,1)}) %all-gather.8.cloned.1.call-update) | async-done | bytes 1572880 | tf_op jit(solution)/shard_map/all_gather | solution.py:168
  108.6 8.9 %fusion.59 = f32[384,2048]{1,0:T(8,128)} fusion(bf16[384,2048]{1,0:T(8,128)(2,1)} %all-gather.8.cloned.1.call-done, bf16[2048,2048]{1,0:T(8,128)(2,1)} %param.23), kind=kOutput, calls=%fused_computation.102 | convolution fusion | flops 3221225472 | bytes 13107200 | tf_op jit(solution)/shard_map/dot_general | solution.py:167
  117.5 0.0 reduce-scatter.2.cloned.1.call-update
  117.5 60.4 %reduce-scatter.2.cloned.1.call-done = f32[96,2048]{1,0:T(8,128)} async-done(((f32[384,2048]{1,0:T(8,128)}), f32[96,2048]{1,0:T(8,128)}) %reduce-scatter.2.cloned.1.call-update) | async-done | bytes 786448 | tf_op jit(solution)/shard_map/reduce_scatter | solution.py:172
  178.0 1.2 convert_element_type.35
  179.2 1.1 collective-permute-start
  180.3 11.5 %collective-permute-done = bf16[96,2048]{1,0:T(8,128)(2,1)S(1)} collective-permute-done((bf16[96,2048]{1,0:T(8,128)(2,1)S(1)}, bf16[96,2048]{1,0:T(8,128)(2,1)S(1)}, u32[]{:S(2)}, u32[]{:S(2)}) %collective-permute-start) | collective-permute-done | bytes 393248 | tf_op jit(solution)/shard_map/ppermute | solution.py:177
  191.8 11.6 %collective-permute-done.1 = bf16[96,2048]{1,0:T(8,128)(2,1)S(1)} collective-permute-done((bf16[96,2048]{1,0:T(8,128)(2,1)S(1)}, bf16[96,2048]{1,0:T(8,128)(2,1)S(1)}, u32[]{:S(2)}, u32[]{:S(2)}) %collective-permute-start.1) | collective-permute-done | bytes 393248 | tf_op jit(solution)/shard_map/ppermute | solution.py:177
  203.4 10.7 %collective-permute-done.2 = bf16[96,2048]{1,0:T(8,128)(2,1)S(1)} collective-permute-done((bf16[96,2048]{1,0:T(8,128)(2,1)S(1)}, bf16[96,2048]{1,0:T(8,128)(2,1)S(1)}, u32[]{:S(2)}, u32[]{:S(2)}) %collective-permute-start.2) | collective-permute-done | bytes 393248 | tf_op jit(solution)/shard_map/ppermute | solution.py:177
  214.3 0.5 constant_dynamic-slice_fusion
  214.8 0.1 slice.12
  214.9 0.8 copy_bitcast_fusion
  215.7 1.0 copy.99
  (51 shorter events, 0.6 us)
Async XLA Ops:
  7.2 1.1 copy-start
  7.2 32.9 %all-gather.4.cloned.1.call-start = ((), (), s32[]{:S(2)}) async-start(), calls=%async_computation.1 | async-start | bytes 2621440 | tf_op jit(solution)/shard_map/all_gather | solution.py:127
  9.8 5.6 %copy-start.8 = (bf16[2,32,2,128]{3,2,1,0:T(2,128)(2,1)S(1)}, bf16[2,32,2,128]{3,2,1,0:T(2,128)(2,1)}, u32[]{:S(2)}) copy-start(bf16[2,32,2,128]{3,2,1,0:T(2,128)(2,1)} %param.14) | copy-start | bytes 98308
  9.8 12.1 %copy-start.7 = (bf16[4,8,16,128]{3,2,1,0:T(8,128)(2,1)S(1)}, bf16[4,8,16,128]{3,2,1,0:T(8,128)(2,1)}, u32[]{:S(2)}) copy-start(bf16[4,8,16,128]{3,2,1,0:T(8,128)(2,1)} %param.19) | copy-start | bytes 393220
  12.5 9.8 %copy-start.9 = (bf16[2,32,2,128]{3,2,1,0:T(2,128)(2,1)S(1)}, bf16[2,32,2,128]{3,2,1,0:T(2,128)(2,1)}, u32[]{:S(2)}) copy-start(bf16[2,32,2,128]{3,2,1,0:T(2,128)(2,1)} %param.15) | copy-start | bytes 98308
  13.5 14.7 %copy-start.5 = (bf16[2,32,16,128]{3,2,1,0:T(8,128)(2,1)S(1)}, bf16[2,32,16,128]{3,2,1,0:T(8,128)(2,1)}, u32[]{:S(2)}) copy-start(bf16[2,32,16,128]{3,2,1,0:T(8,128)(2,1)} %param.13) | copy-start | bytes 786436
  13.6 15.5 %copy-start.13 = (s32[32]{0:T(128)S(1)}, s32[32]{0:T(128)}, u32[]{:S(2)}) copy-start(s32[32]{0:T(128)} %param.22) | copy-start | bytes 388
  13.6 16.1 %copy-start.11 = (bf16[4,8,2,128]{3,2,1,0:T(2,128)(2,1)S(1)}, bf16[4,8,2,128]{3,2,1,0:T(2,128)(2,1)}, u32[]{:S(2)}) copy-start(bf16[4,8,2,128]{3,2,1,0:T(2,128)(2,1)} %param.20) | copy-start | bytes 49156
  14.5 50.9 %all-gather.6.cloned.1.call-start = ((), (), s32[]{:S(2)}) async-start(), calls=%async_computation.2 | async-start | bytes 2621440 | tf_op jit(solution)/shard_map/all_gather | solution.py:128
  15.4 93.2 %all-gather.8.cloned.1.call-start = ((), (), s32[]{:S(2)}) async-start(), calls=%async_computation.3 | async-start | bytes 1966080 | tf_op jit(solution)/shard_map/all_gather | solution.py:168
  42.9 3.6 %copy-start.1 = (f32[4,2048,256]{2,1,0:T(8,128)}, f32[4,2048,256]{2,1,0:T(8,128)S(1)}, u32[]{:S(2)}) copy-start(f32[4,2048,256]{2,1,0:T(8,128)S(1)} %get-tuple-element.88) | copy-start | bytes 25165828
  43.0 3.5 %copy-start.2 = (bf16[2,2,2048,128]{3,2,1,0:T(8,128)(2,1)S(1)}, bf16[2,2,2048,128]{3,2,1,0:T(8,128)(2,1)}, u32[]{:S(2)}) copy-start(bf16[2,2,2048,128]{3,2,1,0:T(8,128)(2,1)} %all-gather.4.cloned.1.call-done) | copy-start | bytes 6291460
  72.4 10.1 %copy-start.3 = (bf16[2,2,2048,128]{3,2,1,0:T(8,128)(2,1)S(1)}, bf16[2,2,2048,128]{3,2,1,0:T(8,128)(2,1)}, u32[]{:S(2)}) copy-start(bf16[2,2,2048,128]{3,2,1,0:T(8,128)(2,1)} %all-gather.6.cloned.1.call-done) | copy-start | bytes 6291460
  82.5 4.9 %copy-start.10 = (pred[2,8]{1,0:T(4,128)(4,1)S(1)}, pred[2,8]{1,0:T(4,128)(4,1)}, u32[]{:S(2)}) copy-start(pred[2,8]{1,0:T(4,128)(4,1)} %iota_compare_fusion.2) | copy-start | bytes 52
  82.5 5.0 %copy-start.6 = (f32[2,4,8,8,4]{3,4,1,2,0:T(4,128)S(1)}, f32[2,4,8,8,4]{3,4,1,2,0:T(4,128)}, u32[]{:S(2)}) copy-start(f32[2,4,8,8,4]{3,4,1,2,0:T(4,128)} %get-tuple-element.86) | copy-start | bytes 24580
  82.5 5.0 %copy-start.12 = (bf16[4,8,2,128]{3,2,1,0:T(2,128)(2,1)S(1)}, bf16[4,8,2,128]{3,2,1,0:T(2,128)(2,1)}, u32[]{:S(2)}) copy-start(bf16[4,8,2,128]{3,2,1,0:T(2,128)(2,1)} %param.21) | copy-start | bytes 49156
  88.8 89.2 %reduce-scatter.2.cloned.1.call-start = ((), (), s32[]{:S(2)}) async-start(), calls=%async_computation.4 | async-start | bytes 3932160 | tf_op jit(solution)/shard_map/reduce_scatter | solution.py:172
  177.9 36.2 %copy-start.4 = (f32[96,2048]{1,0:T(8,128)S(1)}, f32[96,2048]{1,0:T(8,128)}, u32[]{:S(2)}) copy-start(f32[96,2048]{1,0:T(8,128)} %reduce-scatter.2.cloned.1.call-done) | copy-start | bytes 2359300
  179.2 12.5 %collective-permute-start = (bf16[96,2048]{1,0:T(8,128)(2,1)S(1)}, bf16[96,2048]{1,0:T(8,128)(2,1)S(1)}, u32[]{:S(2)}, u32[]{:S(2)}) collective-permute-start(bf16[96,2048]{1,0:T(8,128)(2,1)S(1)} %convert_element_type.35), channel_id=1, source_target_pairs={{0,1},{1,2},{2,3},{3,0},{4,5},{5,6},{6,7},{7,4},{8,9},{9,10},{10,1... | collective-permute-start | bytes 1179656 | tf_op jit(solution)/shard_map/ppermute | solution.py:177
  191.8 11.6 %collective-permute-start.1 = (bf16[96,2048]{1,0:T(8,128)(2,1)S(1)}, bf16[96,2048]{1,0:T(8,128)(2,1)S(1)}, u32[]{:S(2)}, u32[]{:S(2)}) collective-permute-start(bf16[96,2048]{1,0:T(8,128)(2,1)S(1)} %collective-permute-done), channel_id=1, source_target_pairs={{0,1},{1,2},{2,3},{3,0},{4,5},{5,6},{6,7},{7,4},{8,9},{9,10},{10,1... | collective-permute-start | bytes 1179656 | tf_op jit(solution)/shard_map/ppermute | solution.py:177
  203.3 10.7 %collective-permute-start.2 = (bf16[96,2048]{1,0:T(8,128)(2,1)S(1)}, bf16[96,2048]{1,0:T(8,128)(2,1)S(1)}, u32[]{:S(2)}, u32[]{:S(2)}) collective-permute-start(bf16[96,2048]{1,0:T(8,128)(2,1)S(1)} %collective-permute-done.1), channel_id=1, source_target_pairs={{0,1},{1,2},{2,3},{3,0},{4,5},{5,6},{6,7},{7,4},{8,9},{9,10},{10,1... | collective-permute-start | bytes 1179656 | tf_op jit(solution)/shard_map/ppermute | solution.py:177
Sparse Core Ops, SparseCore 0:
  14.6 25.4 all-gather.3
  42.2 23.1 all-gather.5
  88.9 19.6 all-gather.7
  117.7 60.2 reduce-scatter.1
